TPU v7x, 128 devices: a whole 4x4x4 slice. The times are simulated.
128 devices in a mesh: req: 16 (over y, z_hi, core), kv: 8 (over z_lo, x).
Axes of the slice: x: 4, y: 4, z: 4 (z_hi: 2, z_lo: 2; z = z_hi * 2 + z_lo), core: 2. Of those that a mesh axis runs over, the one named last changes fastest.
Arguments:
- tokens: bfloat16 [1024, 8192], P(None, 'req'), may hold values from -40 to 40
- norm_in: bfloat16 [8192], P('req'), may hold values from 0.099609375 to 1.8984375
- w_qkv: bfloat16 [8192, 10240], P('req', 'kv'), may hold values from -0.0625 to 0.0625
- qkv_bias: bfloat16 [10240], P('kv'), may hold values from -12 to 12
- w_out: bfloat16 [8192, 8192], P('kv', 'req'), may hold values from -0.0625 to 0.0625
- norm_mid: bfloat16 [8192], P('req'), may hold values from 0.099609375 to 1.8984375
- w_gate: bfloat16 [8192, 29568], P('req', 'kv'), may hold values from -0.0625 to 0.0625
- w_up: bfloat16 [8192, 29568], P('req', 'kv'), may hold values from -0.0625 to 0.0625
- w_down: bfloat16 [29568, 8192], P('kv', 'req'), may hold values from -0.03125 to 0.03125
- short_keys: bfloat16 [1024, 256, 8, 128], P('req', None, 'kv'), may hold values from -310 to 310
- short_values: bfloat16 [1024, 256, 8, 128], P('req', None, 'kv'), may hold values from -6 to 6
- short_len: int32 [1024], P('req'), may hold values from 1 to 256, 131072 in all
- long_keys: bfloat16 [16, 8192, 8, 128], P('req', None, 'kv'), may hold values from -310 to 310
- long_values: bfloat16 [16, 8192, 8, 128], P('req', None, 'kv'), may hold values from -6 to 6
- long_len: int32 [16], replicated, may hold values from 0 to 8192, as said below
- positions: int32 [1024], P('req'), may hold values from 0 to 32767
Outputs:
- layer_out: bfloat16 [1024, 8192], P(None, 'req')
Inputs may be any that keep to these rules, and one draw needn't show every extreme that they name: `short_len`: short lengths sum to 131072 and the largest is 256. `long_len`: exactly 8 segments are live, the others have length 0; live ones hold at least 4096 slots and one holds 8192.
All inputs are finite; a program needn't handle non-finite values. No bound on the sum of `short_len` on one device may be relied on, other than what follows from the above.
Results may differ from a plain program's by a relative error of at most 0.0085.
Values may be sent and summed in bfloat16 or wider, within the bound.
No kernel may reach another device: no remote copies, remote signals or barrier semaphores. Data moves between devices by JAX's collectives and lax.ppermute only.
A program may use at most 128 MiB of HBM per device.

v0:
```python
import jax
import jax.numpy as jnp
from jax import lax
from jax.sharding import PartitionSpec as P

D = 8192
HD = 128
SHORT_CAP = 256
LONG_CAP = 8192
REQ_DEV = 64
GROUP = 8
EPS = 1e-06
THETA = 1000000.0
NEGATIVE = -1e30


def rotate(values, angles):
    half = values.shape[-1] // 2
    first = values[..., :half]
    second = values[..., half:]
    cosine = jnp.cos(angles)
    sine = jnp.sin(angles)
    return jnp.concatenate(
        [first * cosine - second * sine, second * cosine + first * sine], axis=-1
    )


def weigh(short_raw, own_raw, short_values, own_values, peak):
    short_weights = jnp.exp(short_raw - peak[..., None])
    own_weights = jnp.exp(own_raw - peak)
    total = jnp.sum(short_weights, axis=3) + own_weights
    summed = jnp.einsum(
        "rhgs,rshd->rhgd",
        short_weights.astype(jnp.bfloat16),
        short_values,
        preferred_element_type=jnp.float32,
    )
    summed = summed + jnp.einsum(
        "rhg,rhd->rhgd",
        own_weights.astype(jnp.bfloat16),
        own_values,
        preferred_element_type=jnp.float32,
    )
    return (total, summed)


def per_device(
    tokens,
    norm_in,
    w_qkv,
    qkv_bias,
    w_out,
    norm_mid,
    w_gate,
    w_up,
    w_down,
    short_keys,
    short_values,
    short_len,
    long_keys,
    long_values,
    long_len,
    positions,
):
    heads_here = short_keys.shape[2]
    scale = HD ** (-0.5)
    wide = tokens.astype(jnp.float32)
    slot = lax.axis_index("req")
    square_in = lax.psum(jnp.sum(wide * wide, axis=1), "req")
    gained = (wide * norm_in.astype(jnp.float32)[None, :]).astype(jnp.bfloat16)
    united = lax.psum_scatter(
        jnp.dot(gained, w_qkv, preferred_element_type=jnp.float32).astype(jnp.bfloat16),
        "req",
        scatter_dimension=0,
        tiled=True,
    ).astype(jnp.float32)
    scale_in = lax.rsqrt(lax.dynamic_slice_in_dim(square_in, slot * REQ_DEV, REQ_DEV) / D + EPS)
    united = (united * scale_in[:, None] + qkv_bias.astype(jnp.float32)[None, :]).reshape(
        REQ_DEV, heads_here, GROUP + 2, HD
    )
    inv_freq = THETA ** (-(2.0 * jnp.arange(HD // 2, dtype=jnp.float32)) / HD)
    angles = positions.astype(jnp.float32)[:, None] * inv_freq[None, :]
    queries = rotate(united[:, :, :GROUP], angles[:, None, None, :]).astype(jnp.bfloat16)
    new_keys = rotate(united[:, :, GROUP], angles[:, None, :]).astype(jnp.bfloat16)
    new_values = united[:, :, GROUP + 1].astype(jnp.bfloat16)
    short_raw = (
        jnp.einsum("rhgd,rshd->rhgs", queries, short_keys, preferred_element_type=jnp.float32)
        * scale
    )
    live = jnp.arange(SHORT_CAP)[None, :] < short_len[:, None]
    short_raw = jnp.where(live[:, None, None, :], short_raw, NEGATIVE)
    own_raw = (
        jnp.einsum("rhgd,rhd->rhg", queries, new_keys, preferred_element_type=jnp.float32) * scale
    )
    peak = jnp.maximum(jnp.max(short_raw, axis=3), own_raw)
    slot_len = lax.dynamic_index_in_dim(long_len, slot, 0, keepdims=False)
    long_raw = (
        jnp.einsum("hgd,lhd->hgl", queries[0], long_keys[0], preferred_element_type=jnp.float32)
        * scale
    )
    long_live = jnp.arange(LONG_CAP) < slot_len
    long_raw = jnp.where(long_live[None, None, :], long_raw, NEGATIVE)
    first_peak = jnp.maximum(peak[0], jnp.max(long_raw, axis=2))
    peak = jnp.concatenate([first_peak[None], peak[1:]], axis=0)
    total, summed = weigh(short_raw, own_raw, short_values, new_values, peak)
    long_weights = jnp.where(
        long_live[None, None, :], jnp.exp(long_raw - first_peak[:, :, None]), 0.0
    )
    long_summed = jnp.einsum(
        "hgl,lhd->hgd",
        long_weights.astype(jnp.bfloat16),
        long_values[0],
        preferred_element_type=jnp.float32,
    )
    total = total.at[0].add(jnp.sum(long_weights, axis=2))
    summed = summed.at[0].add(long_summed)
    attended = (
        (summed / total[..., None]).astype(jnp.bfloat16).reshape(REQ_DEV, heads_here * GROUP * HD)
    )
    out_part = jnp.dot(
        lax.all_gather(attended, "req", axis=0, tiled=True),
        w_out,
        preferred_element_type=jnp.float32,
    )
    projected = lax.psum(out_part.astype(jnp.bfloat16), "kv").astype(jnp.float32)
    residual = lax.optimization_barrier((wide + projected).astype(jnp.bfloat16))
    resid_wide = residual.astype(jnp.float32)
    square_mid = lax.psum(jnp.sum(resid_wide * resid_wide, axis=1), "req")
    mixed_in = (resid_wide * norm_mid.astype(jnp.float32)[None, :]).astype(jnp.bfloat16)
    units = w_gate.shape[1]
    padded = -(-units // 128) * 128
    w_gate_up = jnp.concatenate(
        [
            jnp.pad(w_gate, ((0, 0), (0, padded - units))),
            jnp.pad(w_up, ((0, 0), (0, padded - units))),
        ],
        axis=1,
    )
    gate_up = lax.psum_scatter(
        jnp.dot(mixed_in, w_gate_up, preferred_element_type=jnp.float32).astype(jnp.bfloat16),
        "req",
        scatter_dimension=0,
        tiled=True,
    ).astype(jnp.float32)
    scale_mid = lax.rsqrt(lax.dynamic_slice_in_dim(square_mid, slot * REQ_DEV, REQ_DEV) / D + EPS)
    gate = gate_up[:, :units] * scale_mid[:, None]
    up = gate_up[:, padded : padded + units] * scale_mid[:, None]
    act = (jax.nn.silu(gate) * up).astype(jnp.bfloat16)
    down_part = jnp.dot(
        lax.all_gather(act, "req", axis=0, tiled=True), w_down, preferred_element_type=jnp.float32
    )
    down = lax.psum(down_part.astype(jnp.bfloat16), "kv").astype(jnp.float32)
    return (resid_wide + down).astype(jnp.bfloat16)


def solution(mesh):
    placed = (
        P(None, "req"),
        P("req"),
        P("req", "kv"),
        P("kv"),
        P("kv", "req"),
        P("req"),
        P("req", "kv"),
        P("req", "kv"),
        P("kv", "req"),
        P("req", None, "kv", None),
        P("req", None, "kv", None),
        P("req"),
        P("req", None, "kv", None),
        P("req", None, "kv", None),
        P(),
        P("req"),
    )
    return jax.shard_map(
        per_device, mesh=mesh, in_specs=placed, out_specs=P(None, "req"), check_vma=False
    )
```

profile of v0, /device:TPU:0, one launch (start us, length us, event | category | flops | bytes accessed | tf_op | source)
XLA Modules:
  0.0 543.8 jit_solution(6019344185695769220)
XLA Ops:
  6.5 0.8 convert_element_type.96
  7.4 4.8 convolution_convert_fusion.1
  12.3 0.6 dynamic_slice.11
  12.9 0.3 fusion.15
  13.2 39.1 %psum.28 = f32[1024]{0:T(1024)S(1)} all-reduce(f32[1024]{0:T(1024)S(1)} %fusion.15), channel_id=1, replica_groups=mesh['req'=16,'kv'=8] {'req'}, use_global_device_ids=true, to_apply=%region_2.0 | all-reduce | flops 1024 | bytes 8192 | tf_op jit(solution)/shard_map/psum | solution.py:69
  52.4 0.7 iota_compare_fusion.3
  53.1 0.2 multiply_cosine_fusion.1
  53.3 35.0 %reduce-scatter.3.cloned.1.call-done = bf16[64,1280]{1,0:T(8,128)(2,1)} async-done(((bf16[1024,1280]{1,0:T(8,128)(2,1)}), bf16[64,1280]{1,0:T(8,128)(2,1)}) %reduce-scatter.3.cloned.1.call-update) | async-done | bytes 163856 | tf_op jit(solution)/shard_map/reduce_scatter | solution.py:71
  88.3 1.0 multiply_add_fusion
  89.5 0.2 fusion.70
  89.9 0.8 fusion.84
  90.7 0.3 fusion.67
  91.0 3.5 fusion.83
  94.9 0.3 fusion.51
  95.2 0.2 fusion.47
  95.5 2.9 fusion.29
  98.4 2.0 fusion.38
  100.6 0.7 copy.38
  101.4 47.1 %all-gather.3.cloned.1.call-done = bf16[1024,1024]{1,0:T(8,128)(2,1)} async-done(((bf16[64,1024]{1,0:T(8,128)(2,1)}), bf16[1024,1024]{1,0:T(8,128)(2,1)}) %all-gather.3.cloned.1.call-update) | async-done | bytes 2097168 | tf_op jit(solution)/shard_map/all_gather | solution.py:121
  148.5 4.1 convolution_convert_fusion.3
  152.6 76.1 %all-reduce.5.cloned.1.call-done = bf16[1024,512]{1,0:T(8,128)(2,1)} async-done(((bf16[1024,512]{1,0:T(8,128)(2,1)}), bf16[1024,512]{1,0:T(8,128)(2,1)}) %all-reduce.5.cloned.1.call-update) | async-done | bytes 1048592 | tf_op jit(solution)/shard_map/psum | solution.py:125
  228.8 1.5 fusion.16
  230.3 14.7 %convolution_convert_fusion = bf16[1024,7424]{1,0:T(8,128)(2,1)} fusion(bf16[512,3696]{0,1:T(8,128)(2,1)} %param.27, bf16[512,3696]{0,1:T(8,128)(2,1)} %param.26, bf16[1024,512]{1,0:T(8,128)(2,1)S(1)} %fusion.16, f32[512]{0:T(512)S(1)} %convert_element_type.110), kind=kOutput, calls=%fused_computation.4 | convolution fusion | flops 7824211968 | bytes 23824384 | tf_op jit(solution)/shard_map/dot_general | solution.py:140
  245.0 0.3 fusion.18
  245.3 33.3 %psum.30 = f32[1024]{0:T(1024)S(1)} all-reduce(f32[1024]{0:T(1024)S(1)} %fusion.18), channel_id=1, replica_groups=mesh['req'=16,'kv'=8] {'req'}, use_global_device_ids=true, to_apply=%region_10.11 | all-reduce | flops 1024 | bytes 8192 | tf_op jit(solution)/shard_map/psum | solution.py:128
  278.7 101.1 %reduce-scatter.5.cloned.1.call-done = bf16[64,7424]{1,0:T(8,128)(2,1)} async-done(((bf16[1024,7424]{1,0:T(8,128)(2,1)}), bf16[64,7424]{1,0:T(8,128)(2,1)}) %reduce-scatter.5.cloned.1.call-update) | async-done | bytes 950288 | tf_op jit(solution)/shard_map/reduce_scatter | solution.py:139
  379.8 1.3 convert_element_type.113
  381.1 1.1 fusion.46
  382.3 67.5 %all-gather.5.cloned.1.call-done = bf16[1024,3696]{1,0:T(8,128)(2,1)} async-done(((bf16[64,3696]{1,0:T(8,128)(2,1)}), bf16[1024,3696]{1,0:T(8,128)(2,1)}) %all-gather.5.cloned.1.call-update) | async-done | bytes 7569424 | tf_op jit(solution)/shard_map/all_gather | solution.py:150
  449.8 9.6 %convolution_convert_fusion.2 = bf16[1024,512]{1,0:T(8,128)(2,1)} fusion(bf16[1024,3696]{1,0:T(8,128)(2,1)} %all-gather.5.cloned.1.call-done, bf16[3696,512]{1,0:T(8,128)(2,1)} %param.28), kind=kOutput, calls=%fused_computation.32 | convolution fusion | flops 3876061184 | bytes 12402688 | tf_op jit(solution)/shard_map/dot_general | solution.py:149
  459.4 75.1 %all-reduce.7.cloned.1.call-done = bf16[1024,512]{1,0:T(8,128)(2,1)} async-done(((bf16[1024,512]{1,0:T(8,128)(2,1)}), bf16[1024,512]{1,0:T(8,128)(2,1)}) %all-reduce.7.cloned.1.call-update) | async-done | bytes 1048592 | tf_op jit(solution)/shard_map/psum | solution.py:152
  534.5 2.5 fusion.19
  (56 shorter events, 1.6 us)
Async XLA Ops:
  6.5 83.4 %copy-start = (bf16[1,8192,1,128]{3,1,2,0:T(8,128)(2,1)S(1)}, bf16[1,8192,1,128]{3,1,2,0:T(8,128)(2,1)}, u32[]{:S(2)}) copy-start(bf16[1,8192,1,128]{3,1,2,0:T(8,128)(2,1)} %param.32) | copy-start | bytes 6291460
  6.5 81.8 %reduce-scatter.3.cloned.1.call-start = ((), (), s32[]{:S(2)}) async-start(), calls=%async_computation.2 | async-start | bytes 2785280 | tf_op jit(solution)/shard_map/reduce_scatter | solution.py:71
  7.4 4.9 copy-start.7
  7.4 4.9 copy-start.4
  7.4 4.9 copy-start.8
  7.4 5.5 %copy-start.2 = (bf16[1024,512]{1,0:T(8,128)(2,1)S(1)}, bf16[1024,512]{1,0:T(8,128)(2,1)}, u32[]{:S(2)}) copy-start(bf16[1024,512]{1,0:T(8,128)(2,1)} %param.20) | copy-start | bytes 3145732
  7.4 45.7 %copy-start.6 = (s32[64]{0:T(128)S(1)}, s32[64]{0:T(128)}, u32[]{:S(2)}) copy-start(s32[64]{0:T(128)} %param.31) | copy-start | bytes 772
  12.2 136.3 %all-gather.3.cloned.1.call-start = ((), (), s32[]{:S(2)}) async-start(), calls=%async_computation.3 | async-start | bytes 2228224 | tf_op jit(solution)/shard_map/all_gather | solution.py:121
  101.3 51.3 %copy-start.5 = (bf16[512]{0:T(512)(128)(2,1)S(1)}, bf16[512]{0:T(512)(128)(2,1)}, u32[]{:S(2)}) copy-start(bf16[512]{0:T(512)(128)(2,1)} %param.25) | copy-start | bytes 3076
  101.3 127.5 %copy-start.3 = (bf16[1024,512]{1,0:T(8,128)(2,1)S(1)}, bf16[1024,512]{1,0:T(8,128)(2,1)}, u32[]{:S(2)}) copy-start(bf16[1024,512]{1,0:T(8,128)(2,1)} %param.20) | copy-start | bytes 3145732
  101.3 127.4 %all-reduce.5.cloned.1.call-start = ((), (), s32[]{:S(2)}) async-start(), calls=%async_computation.4 | async-start | bytes 2097152 | tf_op jit(solution)/shard_map/psum | solution.py:125
  152.6 227.3 %reduce-scatter.5.cloned.1.call-start = ((), (), s32[]{:S(2)}) async-start(), calls=%async_computation.5 | async-start | bytes 16154624 | tf_op jit(solution)/shard_map/reduce_scatter | solution.py:139
  245.0 204.8 %all-gather.5.cloned.1.call-start = ((), (), s32[]{:S(2)}) async-start(), calls=%async_computation.6 | async-start | bytes 8077312 | tf_op jit(solution)/shard_map/all_gather | solution.py:150
  382.3 152.2 %all-reduce.7.cloned.1.call-start = ((), (), s32[]{:S(2)}) async-start(), calls=%async_computation.7 | async-start | bytes 2097152 | tf_op jit(solution)/shard_map/psum | solution.py:152
  449.8 87.2 %copy-start.1 = (bf16[1,8192,1,128]{3,1,2,0:T(8,128)(2,1)S(1)}, bf16[1,8192,1,128]{3,1,2,0:T(8,128)(2,1)}, u32[]{:S(2)}) copy-start(bf16[1,8192,1,128]{3,1,2,0:T(8,128)(2,1)} %param.32) | copy-start | bytes 6291460
Sparse Core Ops, SparseCore 0:
  12.3 75.9 reduce-scatter.2
  101.4 47.0 all-gather.2
  152.7 76.0 all-reduce.4
  245.1 134.6 reduce-scatter.4
  382.4 67.3 all-gather.4
  459.5 74.9 all-reduce.6
where the time goes:
time: 544 us
  waiting for transfers between devices  402 us (74%)
  blocking collectives  72.5 us (13%)
  matrix products  42.6 us (8%)
  between operations  13.8 us (3%)
  other arithmetic  11.2 us (2%)
    reduce_scatter x1, waiting for transfers between devices, per_device(): lax.psum_scatter(jnp.dot(mixed_in, w_gate_up, preferred_element_type=jnp....  101 us
    psum x1, waiting for transfers between devices, per_device(): lax.psum(out_part.astype(jnp.bfloat16), 'kv').astype(jnp.float32)  76.1 us
    psum x1, waiting for transfers between devices, per_device(): down = lax.psum(down_part.astype(jnp.bfloat16), 'kv').astype(jnp.float32)  75.1 us
    all_gather x1, waiting for transfers between devices, per_device(): lax.all_gather(act, 'req', axis=0, tiled=True)  67.5 us
    all_gather x1, waiting for transfers between devices, per_device(): lax.all_gather(attended, 'req', axis=0, tiled=True)  47.1 us
    psum x1, blocking collectives, per_device(): square_in = lax.psum(jnp.sum(wide * wide, axis=1), 'req')  39.1 us
    reduce_scatter x1, waiting for transfers between devices, per_device(): lax.psum_scatter(jnp.dot(gained, w_qkv, preferred_element_type=jnp.float3...  35 us
    psum x1, blocking collectives, per_device(): square_mid = lax.psum(jnp.sum(resid_wide * resid_wide, axis=1), 'req')  33.3 us
  transfers between devices with their start and end apart: 6, of which 6 were waited for; matrix products, arithmetic and copies ran while one was open for 0% of the time, Pallas kernels for 0%

commit v1 on v0

--- a/solution.py
+++ b/solution.py
@@ -1,3 +1,4 @@
+import functools
 import jax
 import jax.numpy as jnp
 from jax import lax
@@ -12,6 +13,21 @@
 EPS = 1e-06
 THETA = 1000000.0
 NEGATIVE = -1e30
+
+
+def play_leaves(target, lane_axis):
+    return jnp.concatenate(
+        lax.all_to_all(
+            jnp.stack([target for _ in range(lax.axis_size(lane_axis))], axis=0),
+            lane_axis,
+            concat_axis=0,
+            split_axis=0,
+        ),
+        axis=0,
+    )
+
+
+_set_patches = functools.partial(play_leaves, lane_axis="req")
 
 
 def rotate(values, angles):
@@ -117,11 +133,7 @@
     attended = (
         (summed / total[..., None]).astype(jnp.bfloat16).reshape(REQ_DEV, heads_here * GROUP * HD)
     )
-    out_part = jnp.dot(
-        lax.all_gather(attended, "req", axis=0, tiled=True),
-        w_out,
-        preferred_element_type=jnp.float32,
-    )
+    out_part = jnp.dot(_set_patches(attended), w_out, preferred_element_type=jnp.float32)
     projected = lax.psum(out_part.astype(jnp.bfloat16), "kv").astype(jnp.float32)
     residual = lax.optimization_barrier((wide + projected).astype(jnp.bfloat16))
     resid_wide = residual.astype(jnp.float32)

time: 544 us -> 526 us (0.967)
  waiting for transfers between devices: 402 us -> 353 us
  blocking collectives: 72.5 us -> 106 us
    all_gather x1 -> x0, waiting for transfers between devices: 47.1 us -> none  [per_device(): lax.all_gather(attended, 'req', axis=0, tiled=True)]
    all_to_all x0 -> x1, blocking collectives: none -> 33.5 us  [play_leaves(): lax.all_to_all(jnp.stack([target for _ in range(lax.axis_size(lane_axis))...]
  transfers between devices with their start and end apart: 6 -> 5, of which waited for: 6 -> 5; matrix products, arithmetic and copies ran while one was open for 0% -> 0% of each run, Pallas kernels for 0% -> 0%
where the time goes in v1:
time: 526 us
  waiting for transfers between devices  353 us (67%)
  blocking collectives  106 us (20%)
  matrix products  40.7 us (8%)
  between operations  13.4 us (3%)
  other arithmetic  11.2 us (2%)
    reduce_scatter x1, waiting for transfers between devices, per_device(): lax.psum_scatter(jnp.dot(mixed_in, w_gate_up, preferred_element_type=jnp....  101 us
    psum x1, waiting for transfers between devices, per_device(): down = lax.psum(down_part.astype(jnp.bfloat16), 'kv').astype(jnp.float32)  75.1 us
    psum x1, waiting for transfers between devices, per_device(): lax.psum(out_part.astype(jnp.bfloat16), 'kv').astype(jnp.float32)  74.2 us
    all_gather x1, waiting for transfers between devices, per_device(): lax.all_gather(act, 'req', axis=0, tiled=True)  67.5 us
    psum x1, blocking collectives, per_device(): square_in = lax.psum(jnp.sum(wide * wide, axis=1), 'req')  39.1 us
    reduce_scatter x1, waiting for transfers between devices, per_device(): lax.psum_scatter(jnp.dot(gained, w_qkv, preferred_element_type=jnp.float3...  35 us
    all_to_all x1, blocking collectives, play_leaves(): lax.all_to_all(jnp.stack([target for _ in range(lax.axis_size(lane_axis))...  33.5 us
    psum x1, blocking collectives, per_device(): square_mid = lax.psum(jnp.sum(resid_wide * resid_wide, axis=1), 'req')  33.2 us
  transfers between devices with their start and end apart: 5, of which 5 were waited for; matrix products, arithmetic and copies ran while one was open for 0% of the time, Pallas kernels for 0%

profile of v1, /device:TPU:0, one launch (start us, length us, event | category | flops | bytes accessed | tf_op | source)
XLA Modules:
  0.0 525.6 jit_solution(1256387426290898459)
XLA Ops:
  6.5 0.8 convert_element_type.96
  7.4 4.8 convolution_convert_fusion.1
  12.3 0.6 dynamic_slice.11
  12.9 0.3 fusion.15
  13.2 39.1 %psum.28 = f32[1024]{0:T(1024)S(1)} all-reduce(f32[1024]{0:T(1024)S(1)} %fusion.15), channel_id=1, replica_groups=mesh['req'=16,'kv'=8] {'req'}, use_global_device_ids=true, to_apply=%region_2.0 | all-reduce | flops 1024 | bytes 8192 | tf_op jit(solution)/shard_map/psum | solution.py:85
  52.4 0.7 iota_compare_fusion.3
  53.3 35.0 %reduce-scatter.3.cloned.1.call-done = bf16[64,1280]{1,0:T(8,128)(2,1)} async-done(((bf16[1024,1280]{1,0:T(8,128)(2,1)}), bf16[64,1280]{1,0:T(8,128)(2,1)}) %reduce-scatter.3.cloned.1.call-update) | async-done | bytes 163856 | tf_op jit(solution)/shard_map/reduce_scatter | solution.py:87
  88.3 1.0 multiply_add_fusion
  89.5 0.2 fusion.70
  89.9 0.8 fusion.84
  90.7 0.3 fusion.67
  91.0 3.5 fusion.83
  94.9 0.3 fusion.51
  95.2 0.2 fusion.47
  95.5 2.9 fusion.29
  98.4 2.0 fusion.38
  100.6 0.3 stack.3
  100.9 33.5 %all_to_all.5 = bf16[16,64,1024]{2,1,0:T(8,128)(2,1)S(1)} all-to-all(bf16[16,64,1024]{2,1,0:T(8,128)(2,1)S(1)} %stack.3), channel_id=1, replica_groups=mesh['req'=16,'kv'=8] {'req'}, dimensions={0} | all-to-all | bytes 4194304 | tf_op jit(solution)/shard_map/all_to_all | solution.py:20
  134.4 2.2 convolution_convert_fusion.3
  136.7 74.2 %all-reduce.5.cloned.1.call-done = bf16[1024,512]{1,0:T(8,128)(2,1)} async-done(((bf16[1024,512]{1,0:T(8,128)(2,1)}), bf16[1024,512]{1,0:T(8,128)(2,1)}) %all-reduce.5.cloned.1.call-update) | async-done | bytes 1048592 | tf_op jit(solution)/shard_map/psum | solution.py:137
  210.9 1.5 fusion.16
  212.4 14.7 %convolution_convert_fusion = bf16[1024,7424]{1,0:T(8,128)(2,1)} fusion(bf16[512,3696]{0,1:T(8,128)(2,1)} %param.27, bf16[512,3696]{0,1:T(8,128)(2,1)} %param.26, bf16[1024,512]{1,0:T(8,128)(2,1)S(1)} %fusion.16, f32[512]{0:T(512)S(1)} %convert_element_type.110), kind=kOutput, calls=%fused_computation.4 | convolution fusion | flops 7824211968 | bytes 23824384 | tf_op jit(solution)/shard_map/dot_general | solution.py:152
  227.1 0.2 all-gather.2.cloned.1.call-start
  227.3 0.3 fusion.18
  227.6 33.2 %psum.30 = f32[1024]{0:T(1024)S(1)} all-reduce(f32[1024]{0:T(1024)S(1)} %fusion.18), channel_id=1, replica_groups=mesh['req'=16,'kv'=8] {'req'}, use_global_device_ids=true, to_apply=%region_10.11 | all-reduce | flops 1024 | bytes 8192 | tf_op jit(solution)/shard_map/psum | solution.py:140
  260.9 101.0 %reduce-scatter.5.cloned.1.call-done = bf16[64,7424]{1,0:T(8,128)(2,1)} async-done(((bf16[1024,7424]{1,0:T(8,128)(2,1)}), bf16[64,7424]{1,0:T(8,128)(2,1)}) %reduce-scatter.5.cloned.1.call-update) | async-done | bytes 950288 | tf_op jit(solution)/shard_map/reduce_scatter | solution.py:151
  361.9 1.3 convert_element_type.113
  363.2 1.1 fusion.46
  364.4 67.5 %all-gather.2.cloned.1.call-done = bf16[1024,3696]{1,0:T(8,128)(2,1)} async-done(((bf16[64,3696]{1,0:T(8,128)(2,1)}), bf16[1024,3696]{1,0:T(8,128)(2,1)}) %all-gather.2.cloned.1.call-update) | async-done | bytes 7569424 | tf_op jit(solution)/shard_map/all_gather | solution.py:162
  431.9 9.6 %convolution_convert_fusion.2 = bf16[1024,512]{1,0:T(8,128)(2,1)} fusion(bf16[1024,3696]{1,0:T(8,128)(2,1)} %all-gather.2.cloned.1.call-done, bf16[3696,512]{1,0:T(8,128)(2,1)} %param.28), kind=kOutput, calls=%fused_computation.32 | convolution fusion | flops 3876061184 | bytes 12402688 | tf_op jit(solution)/shard_map/dot_general | solution.py:161
  441.5 75.1 %all-reduce.7.cloned.1.call-done = bf16[1024,512]{1,0:T(8,128)(2,1)} async-done(((bf16[1024,512]{1,0:T(8,128)(2,1)}), bf16[1024,512]{1,0:T(8,128)(2,1)}) %all-reduce.7.cloned.1.call-update) | async-done | bytes 1048592 | tf_op jit(solution)/shard_map/psum | solution.py:164
  516.6 2.5 fusion.19
  (57 shorter events, 1.7 us)
Async XLA Ops:
  6.5 83.4 %copy-start = (bf16[1,8192,1,128]{3,1,2,0:T(8,128)(2,1)S(1)}, bf16[1,8192,1,128]{3,1,2,0:T(8,128)(2,1)}, u32[]{:S(2)}) copy-start(bf16[1,8192,1,128]{3,1,2,0:T(8,128)(2,1)} %param.32) | copy-start | bytes 6291460
  6.5 81.8 %reduce-scatter.3.cloned.1.call-start = ((), (), s32[]{:S(2)}) async-start(), calls=%async_computation.3 | async-start | bytes 2785280 | tf_op jit(solution)/shard_map/reduce_scatter | solution.py:87
  7.4 4.9 copy-start.8
  7.4 4.9 copy-start.4
  7.4 4.9 copy-start.9
  7.4 5.5 %copy-start.2 = (bf16[1024,512]{1,0:T(8,128)(2,1)S(1)}, bf16[1024,512]{1,0:T(8,128)(2,1)}, u32[]{:S(2)}) copy-start(bf16[1024,512]{1,0:T(8,128)(2,1)} %param.20) | copy-start | bytes 3145732
  7.4 45.7 %copy-start.6 = (s32[64]{0:T(128)S(1)}, s32[64]{0:T(128)}, u32[]{:S(2)}) copy-start(s32[64]{0:T(128)} %param.31) | copy-start | bytes 772
  12.2 198.7 %all-reduce.5.cloned.1.call-start = ((), (), s32[]{:S(2)}) async-start(), calls=%async_computation.4 | async-start | bytes 2097152 | tf_op jit(solution)/shard_map/psum | solution.py:137
  100.4 33.9 %copy-start.7 = (bf16[1024,512]{1,0:T(8,128)(2,1)S(1)}, bf16[1024,512]{1,0:T(8,128)(2,1)}, u32[]{:S(2)}) copy-start(bf16[1024,512]{1,0:T(8,128)(2,1)} %param.24) | copy-start | bytes 3145732
  134.4 2.3 copy-start.5
  134.4 76.5 %copy-start.3 = (bf16[1024,512]{1,0:T(8,128)(2,1)S(1)}, bf16[1024,512]{1,0:T(8,128)(2,1)}, u32[]{:S(2)}) copy-start(bf16[1024,512]{1,0:T(8,128)(2,1)} %param.20) | copy-start | bytes 3145732
  136.6 225.3 %reduce-scatter.5.cloned.1.call-start = ((), (), s32[]{:S(2)}) async-start(), calls=%async_computation.5 | async-start | bytes 16154624 | tf_op jit(solution)/shard_map/reduce_scatter | solution.py:151
  227.1 204.8 %all-gather.2.cloned.1.call-start = ((), (), s32[]{:S(2)}) async-start(), calls=%async_computation.6 | async-start | bytes 8077312 | tf_op jit(solution)/shard_map/all_gather | solution.py:162
  364.3 152.3 %all-reduce.7.cloned.1.call-start = ((), (), s32[]{:S(2)}) async-start(), calls=%async_computation.7 | async-start | bytes 2097152 | tf_op jit(solution)/shard_map/psum | solution.py:164
  431.9 87.2 %copy-start.1 = (bf16[1,8192,1,128]{3,1,2,0:T(8,128)(2,1)S(1)}, bf16[1,8192,1,128]{3,1,2,0:T(8,128)(2,1)}, u32[]{:S(2)}) copy-start(bf16[1,8192,1,128]{3,1,2,0:T(8,128)(2,1)} %param.32) | copy-start | bytes 6291460
Sparse Core Ops, SparseCore 0:
  12.3 75.9 reduce-scatter.2
  136.7 74.1 all-reduce.4
  227.2 134.6 reduce-scatter.4
  364.5 67.4 all-gather.1
  441.6 74.9 all-reduce.6
